TPU v7x, 128 devices: a whole 4x4x4 slice. The times are simulated.
128 devices in a mesh: half: 2 (over core), row: 8 (over z_hi, x), col: 8 (over y, z_lo).
Axes of the slice: x: 4, y: 4, z: 4 (z_hi: 2, z_lo: 2; z = z_hi * 2 + z_lo), core: 2. Of those that a mesh axis runs over, the one named last changes fastest.
Arguments:
- child_diag: float32 [2, 512, 512], P('half'), as said below
- child_panel: float32 [2, 16, 8, 128, 512], P('half', None, 'row'), may hold values from -18 to 18
- child_window: float32 [2, 16, 8, 128, 8, 8, 128], P('half', None, 'row', None, None, 'col'), may hold values from -6 to 6
- parent_diag: float32 [512, 512], replicated
- parent_lead_panel: float32 [24, 8, 2, 8, 8, 512], P(None, 'row', 'half', 'col'), may hold values from -24 to 24
- index_maps: int32 [2, 128], replicated, may hold values from 0 to 191, as said below
Outputs:
- parent_front: float32 [24, 8, 128, 4, 2, 8, 128], P(None, 'row', None, None, 'half', 'col')
- parent_factor: float32 [24, 8, 2, 8, 8, 512], P(None, 'row', 'half', 'col')
- parent_pivot: float32 [512, 512], replicated
Inputs may be any that keep to these rules, and one draw needn't show every extreme that they name: child_diag and parent_diag are symmetric and positive definite. For each child k and each group a, the entries index_maps[k, a * 16 + u] with 0 <= u < 16 equal q * 16 + ((u + s) mod 16) for a group target q and a turn s fixed within the group; groups a < 4 have q = a, later groups have distinct q that rise with a; over the 8 groups of a child the turns s, taken modulo 8, are all different; for each child some group a < 4 has a turn divisible by 8, and another group a < 4 has a turn that leaves 1 modulo 8.
All inputs are finite; a program needn't handle non-finite values.
Results may differ from a plain program's by a relative error of at most 0.0001.
Values sent between devices are 32-bit elements; how exact they have to be, the bound alone decides.
No kernel may reach another device: no remote copies, remote signals or barrier semaphores. Data moves between devices by JAX's collectives and lax.ppermute only.
A program may use at most 192 MiB of HBM per device.

v0:
```python
import jax
import jax.numpy as jnp
from jax import lax
from jax.sharding import PartitionSpec as P

BLOCK_EXTENT = 128
PB = 4
SB = 128
RB = 192
WB = 64


def from_root(shard, axis, root):
    mine = lax.axis_index(axis) == root
    return lax.psum(jnp.where(mine, shard, jnp.zeros_like(shard)), axis)


def pick_ranked(owners, values, wanted, slot_count, missing):
    matches = owners[..., None, :] == wanted[:, None]
    ranking = jnp.cumsum(matches.astype(jnp.int32), axis=-1) - 1
    slot_ids = jnp.arange(slot_count, dtype=jnp.int32)
    chosen = matches[..., None, :] & (ranking[..., None, :] == slot_ids[:, None])
    present = jnp.any(chosen, axis=-1)
    picked = jnp.sum(jnp.where(chosen, values[..., None, None, :], 0), axis=-1)
    return jnp.where(present, picked, missing)


def per_device(child_diag, child_panel, child_window, parent_diag, parent_lead_panel, index_maps):
    highest = lax.Precision.HIGHEST
    row_size = lax.axis_size("row")
    half_id = lax.axis_index("half")
    row_id = lax.axis_index("row")
    col_id = lax.axis_index("col")
    panel_width = PB * BLOCK_EXTENT
    group_size = 2 * row_size
    row_local = SB // row_size
    col_local = WB // row_size
    parent_row_blocks = RB // row_size
    parent_cols = WB // group_size
    per_row = 2 * (SB // group_size) // row_size
    per_col = (WB // group_size + row_size - 1) // row_size
    pivot_lower_factor = jnp.linalg.cholesky(parent_diag)
    own_rows = parent_lead_panel.reshape(-1, panel_width)
    solved = jax.scipy.linalg.solve_triangular(pivot_lower_factor, own_rows.T, lower=True).T
    parent_factor = solved.reshape(parent_lead_panel.shape)
    sub_rows = parent_lead_panel.shape[4]
    gathered = lax.all_gather(
        solved.reshape(parent_row_blocks, sub_rows, panel_width),
        ("half", "col"),
        axis=1,
        tiled=True,
    )
    paired = gathered[: 2 * parent_cols].reshape(parent_cols, 2, BLOCK_EXTENT, panel_width)
    offered = lax.dynamic_index_in_dim(paired, half_id, axis=1, keepdims=False)
    column_factor = from_root(offered, "row", col_id)
    child_low = jnp.linalg.cholesky(child_diag[0])
    child_rows = child_panel.reshape(-1, panel_width)
    child_factor = jax.scipy.linalg.solve_triangular(child_low, child_rows.T, lower=True).T
    leading = child_factor[: col_local * BLOCK_EXTENT]
    everyone = lax.all_gather(leading[None], "row", axis=0, tiled=True)
    child_columns = lax.dynamic_index_in_dim(everyone, col_id, axis=0, keepdims=False)
    schur_part = child_window.reshape(row_local * BLOCK_EXTENT, col_local * BLOCK_EXTENT) - jnp.dot(
        child_factor, child_columns.T, precision=highest
    )
    schur_blocks = schur_part.reshape(row_local, BLOCK_EXTENT, col_local, BLOCK_EXTENT)
    child_map = lax.dynamic_index_in_dim(index_maps, half_id, axis=0, keepdims=False)
    my_rows = lax.dynamic_index_in_dim(
        child_map.reshape(row_local, row_size), row_id, axis=1, keepdims=False
    )
    my_cols = lax.dynamic_index_in_dim(
        child_map[:WB].reshape(col_local, row_size), col_id, axis=1, keepdims=False
    )
    local_rows = jnp.arange(row_local, dtype=jnp.int32)
    local_cols = jnp.arange(col_local, dtype=jnp.int32)
    send_rows = pick_ranked(
        my_rows % row_size, local_rows, jnp.arange(row_size, dtype=jnp.int32), per_row, row_local
    )
    send_cols = pick_ranked(
        my_cols % group_size,
        local_cols,
        jnp.arange(group_size, dtype=jnp.int32),
        per_col,
        col_local,
    )
    all_rows = index_maps.reshape(2, row_local, row_size).transpose(0, 2, 1)
    row_target = pick_ranked(
        all_rows % row_size, all_rows // row_size, row_id[None], per_row, parent_row_blocks
    )[:, :, 0, :]
    all_cols = index_maps[:, :WB].reshape(2, col_local, row_size).transpose(0, 2, 1)
    col_target = pick_ranked(
        all_cols % group_size,
        all_cols // group_size,
        (half_id * row_size + col_id)[None],
        per_col,
        parent_cols,
    )[:, :, 0, :]
    assembled_front = jnp.zeros(
        (parent_row_blocks, BLOCK_EXTENT, parent_cols, BLOCK_EXTENT), jnp.float32
    )
    row_index = send_rows[None, :, None, :, None]
    col_index = send_cols.reshape(2, row_size, per_col)[:, None, :, None, :]
    outgoing = schur_blocks.at[row_index, :, col_index, :].get(mode="fill", fill_value=0.0)
    arrived = lax.all_to_all(
        outgoing.reshape(-1, per_row * per_col, BLOCK_EXTENT, BLOCK_EXTENT),
        ("half", "row", "col"),
        split_axis=0,
        concat_axis=0,
        tiled=True,
    )
    arrived = arrived.reshape(2, row_size, row_size, per_row, per_col, BLOCK_EXTENT, BLOCK_EXTENT)
    target_rows = row_target[:, :, None, :, None]
    target_cols = col_target[:, None, :, None, :]
    assembled_front = assembled_front.at[target_rows, :, target_cols, :].add(arrived, mode="drop")
    flat_front = assembled_front.reshape(
        parent_row_blocks * BLOCK_EXTENT, parent_cols * BLOCK_EXTENT
    )
    updated = flat_front - jnp.dot(
        gathered.reshape(-1, panel_width),
        column_factor.reshape(-1, panel_width).T,
        precision=highest,
    )
    return (
        updated.reshape(parent_row_blocks, 1, BLOCK_EXTENT, parent_cols, 1, 1, BLOCK_EXTENT),
        parent_factor,
        pivot_lower_factor,
    )


def solution(mesh):
    in_specs = (
        P("half", None, None),
        P("half", None, "row", None, None),
        P("half", None, "row", None, None, "col", None),
        P(),
        P(None, "row", "half", "col", None, None),
        P(),
    )
    out_specs = (
        P(None, "row", None, None, "half", "col", None),
        P(None, "row", "half", "col", None, None),
        P(),
    )
    return jax.shard_map(
        per_device, mesh=mesh, in_specs=in_specs, out_specs=out_specs, check_vma=False
    )
```

profile of v0, /device:TPU:0, one launch (start us, length us, event | category | flops | bytes accessed | tf_op | source)
XLA Modules:
  0.0 819.9 jit_solution(16038382859682363218)
XLA Ops:
  8.1 5.4 copy.74
  14.1 11.7 %cholesky.286 = f32[128,128]{1,0:T(8,128)S(1)} custom-call(f32[128,128]{1,0:T(8,128)S(1)} %cholesky.426), custom_call_target="Cholesky" | custom-call | tf_op jit(solution)/shard_map/jit(cholesky)/cholesky | solution.py:56
  26.0 9.8 %custom-call.37 = f32[1,128,128]{1,2,0:T(8,128)S(1)} custom-call(f32[1,128,128]{2,1,0:T(8,128)S(1)} %get-tuple-element.91), custom_call_target="InvertDiagBlocksLowerTriangular" | custom-call | tf_op jit(solution)/shard_map/jit(cholesky)/cholesky | solution.py:56
  36.5 11.7 %cholesky.305 = f32[128,128]{1,0:T(8,128)S(1)} custom-call(f32[128,128]{1,0:T(8,128)S(1)} %cholesky.430), custom_call_target="Cholesky" | custom-call | tf_op jit(solution)/shard_map/jit(cholesky)/cholesky | solution.py:56
  48.2 10.2 %custom-call.38 = f32[1,128,128]{1,2,0:T(8,128)S(1)} custom-call(f32[1,128,128]{2,1,0:T(8,128)S(1)} %get-tuple-element.88), custom_call_target="InvertDiagBlocksLowerTriangular" | custom-call | tf_op jit(solution)/shard_map/jit(cholesky)/cholesky | solution.py:56
  59.1 11.7 %cholesky.326 = f32[128,128]{1,0:T(8,128)S(1)} custom-call(f32[128,128]{1,0:T(8,128)S(1)} %cholesky.435), custom_call_target="Cholesky" | custom-call | tf_op jit(solution)/shard_map/jit(cholesky)/cholesky | solution.py:56
  70.9 9.8 %custom-call.39 = f32[1,128,128]{1,2,0:T(8,128)S(1)} custom-call(f32[1,128,128]{2,1,0:T(8,128)S(1)} %get-tuple-element.85), custom_call_target="InvertDiagBlocksLowerTriangular" | custom-call | tf_op jit(solution)/shard_map/jit(cholesky)/cholesky | solution.py:56
  81.3 11.7 %cholesky.343 = f32[128,128]{1,0:T(8,128)S(1)} custom-call(f32[128,128]{1,0:T(8,128)S(1)} %convolution_subtract_fusion.10), custom_call_target="Cholesky" | custom-call | tf_op jit(solution)/shard_map/jit(cholesky)/cholesky | solution.py:56
  97.7 8.7 %while.2 = (s32[]{:T(128)}, f32[512,512]{1,0:T(8,128)S(1)}, s32[4,2]{0,1:T(2,128)S(1)}, f32[4,128,128]{2,1,0:T(8,128)S(1)}, s32[]{:T(128)}) while((s32[]{:T(128)}, f32[512,512]{1,0:T(8,128)S(1)}, s32[4,2]{0,1:T(2,128)S(1)}, f32[4,128,128]{2,1,0:T(8,128)S(1)}, s32[]{:T(128)}) %tuple.70), condition=%wide.while_cond, body=%wide.while_body.sunk | while | flops 2 | bytes 131189 | solution.py:58
  98.6 1.4 bitcast_dynamic-update-slice_fusion.4
  100.7 1.4 bitcast_dynamic-update-slice_fusion.4
  102.8 1.4 bitcast_dynamic-update-slice_fusion.4
  105.0 1.4 bitcast_dynamic-update-slice_fusion.4
  106.4 39.3 %custom-call.28 = f32[4,128,128]{1,2,0:T(8,128)S(1)} custom-call(f32[4,128,128]{2,1,0:T(8,128)S(1)} %get-tuple-element.11), custom_call_target="InvertDiagBlocksLowerTriangular" | custom-call | tf_op jit(solution)/shard_map/jit(_solve_triangular)/triangular_solve | solution.py:58
  145.8 2.4 fusion.16
  148.2 2.2 convolution_subtract_fusion.1
  150.4 1.1 fusion.58
  151.5 1.3 convolution_subtract_fusion
  152.8 1.1 fusion.56
  153.8 3.0 fusion.7
  156.8 1.0 fusion.55
  157.9 1.0 copy-done.1
  159.2 1.6 slice.169
  164.3 2.6 copy.69
  166.8 1.8 fusion.19
  168.6 1.0 copy-done.5
  169.6 11.9 %cholesky.358 = f32[128,128]{1,0:T(8,128)S(1)} custom-call(f32[128,128]{1,0:T(8,128)S(1)} %cholesky.439), custom_call_target="Cholesky" | custom-call | tf_op jit(solution)/shard_map/jit(cholesky)/cholesky | solution.py:42
  181.5 1.1 cholesky.384
  182.6 9.8 %custom-call.40 = f32[1,128,128]{1,2,0:T(8,128)S(1)} custom-call(f32[1,128,128]{2,1,0:T(8,128)S(1)} %get-tuple-element.81), custom_call_target="InvertDiagBlocksLowerTriangular" | custom-call | tf_op jit(solution)/shard_map/jit(cholesky)/cholesky | solution.py:42
  192.5 2.0 constant_dynamic-update-slice_fusion.2
  194.4 1.2 convolution_subtract_fusion.2
  195.7 11.7 %cholesky.377 = f32[128,128]{1,0:T(8,128)S(1)} custom-call(f32[128,128]{1,0:T(8,128)S(1)} %cholesky.443), custom_call_target="Cholesky" | custom-call | tf_op jit(solution)/shard_map/jit(cholesky)/cholesky | solution.py:42
  208.1 9.8 %custom-call.41 = f32[1,128,128]{1,2,0:T(8,128)S(1)} custom-call(f32[1,128,128]{2,1,0:T(8,128)S(1)} %get-tuple-element.78), custom_call_target="InvertDiagBlocksLowerTriangular" | custom-call | tf_op jit(solution)/shard_map/jit(cholesky)/cholesky | solution.py:42
  217.9 0.9 convolution_dynamic-update-slice_fusion
  218.8 1.4 convolution_subtract_fusion.4
  220.2 12.1 %cholesky.398 = f32[128,128]{1,0:T(8,128)S(1)} custom-call(f32[128,128]{1,0:T(8,128)S(1)} %cholesky.448), custom_call_target="Cholesky" | custom-call | tf_op jit(solution)/shard_map/jit(cholesky)/cholesky | solution.py:42
  233.0 9.8 %custom-call.42 = f32[1,128,128]{1,2,0:T(8,128)S(1)} custom-call(f32[1,128,128]{2,1,0:T(8,128)S(1)} %get-tuple-element.75), custom_call_target="InvertDiagBlocksLowerTriangular" | custom-call | tf_op jit(solution)/shard_map/jit(cholesky)/cholesky | solution.py:42
  243.6 1.4 convolution_subtract_fusion.9
  245.1 11.7 %cholesky.415 = f32[128,128]{1,0:T(8,128)S(1)} custom-call(f32[128,128]{1,0:T(8,128)S(1)} %convolution_subtract_fusion.9), custom_call_target="Cholesky" | custom-call | tf_op jit(solution)/shard_map/jit(cholesky)/cholesky | solution.py:42
  260.6 89.0 %all-gather.6.cloned.1.call-done = f32[8192,512]{0,1:T(8,128)} async-done(((f32[1024,512]{0,1:T(8,128)}), f32[8192,512]{0,1:T(8,128)}) %all-gather.6.cloned.1.call-update) | async-done | bytes 16777232 | tf_op jit(solution)/shard_map/all_gather | solution.py:60
  349.5 21.3 %copy.78 = f32[64,8,8,1024]{3,2,1,0:T(8,128)} copy(f32[64,8,8,1024]{3,1,2,0:T(8,128)} %bitcast.224) | data formatting | bytes 33554432
  370.9 9.4 %constant_dynamic-slice_fusion.2 = f32[1,1024,512]{1,0,2:T(1,128)} fusion(f32[8,1024,512]{1,0,2:T(8,128)} %bitcast.223, s32[]{:T(128)S(6)} %select_n.220), kind=kLoop, calls=%fused_computation.208 | loop fusion | bytes 4194308 | tf_op jit(solution)/shard_map/jit(dynamic_index_in_dim)/dynamic_slice | solution.py:61
  380.3 20.5 %fusion = f32[256,8,8,128]{3,1,2,0:T(8,128)S(1)} fusion(f32[256,8,8,128]{3,2,1,0:T(8,128)} %bitcast.231, f32[128,2048]{1,0:T(8,128)} %copy-done.1, f32[128,2048]{1,0:T(8,128)S(1)} %fusion.56, f32[128,2048]{1,0:T(8,128)S(1)} %fusion.58, f32[128,2048]{1,0:T(8,128)S(1)} %fusion.16, f32[1,1024,512]{1,0,2:T(1,128)} %constant_dynamic-slice_fusion.2), kind=kOutput, calls=%fused_computation.7 | convolution fusion | flops 12890144768 | bytes 23068672 | tf_op jit(solution)/shard_map/dot_general | solution.py:62
  400.8 2.1 copy.79
  402.9 4.7 copy.67
  407.6 16.0 %gather_fusion = f32[256,128,128]{2,1,0:T(8,128)} fusion(f32[16,128,8,128]{3,1,2,0:T(8,128)} %copy.67, s32[256]{0:T(256)S(1)} %reshape.575), kind=kCustom, calls=%fused_computation | custom fusion | bytes 33556480 | tf_op jit(solution)/shard_map/gather | solution.py:102
  423.6 11.4 %broadcast_select_fusion = f32[128,2,128,128]{3,2,1,0:T(8,128)} fusion(f32[128,2,128,128]{3,2,1,0:T(8,128)} %bitcast.220, pred[128,2]{1,0:T(8,128)(4,1)S(1)} %bitcast.239), kind=kLoop, calls=%fused_computation.8 | loop fusion | flops 4194304 | bytes 33554688 | tf_op jit(solution)/shard_map/select_n | solution.py:102
  435.0 6.9 all-to-all-start
  443.2 1.2 fusion.20
  444.5 8.5 %while.3 = (s32[]{:T(128)}, f32[512,512]{1,0:T(8,128)S(1)}, s32[4,2]{0,1:T(2,128)S(1)}, f32[4,128,128]{2,1,0:T(8,128)S(1)}, s32[]{:T(128)}) while((s32[]{:T(128)}, f32[512,512]{1,0:T(8,128)S(1)}, s32[4,2]{0,1:T(2,128)S(1)}, f32[4,128,128]{2,1,0:T(8,128)S(1)}, s32[]{:T(128)}) %tuple.82), condition=%wide.while_cond.1, body=%wide.while_body.1.sunk | while | flops 2 | bytes 131189 | solution.py:44
  445.6 1.4 bitcast_dynamic-update-slice_fusion.5
  447.6 1.4 bitcast_dynamic-update-slice_fusion.5
  449.6 1.4 bitcast_dynamic-update-slice_fusion.5
  451.6 1.4 bitcast_dynamic-update-slice_fusion.5
  453.0 39.3 %custom-call.29 = f32[4,128,128]{1,2,0:T(8,128)S(1)} custom-call(f32[4,128,128]{2,1,0:T(8,128)S(1)} %get-tuple-element.19), custom_call_target="InvertDiagBlocksLowerTriangular" | custom-call | tf_op jit(solution)/shard_map/jit(_solve_triangular)/triangular_solve | solution.py:44
  495.5 205.3 %all-gather.4.cloned.1.call-done = f32[24,128,512]{2,1,0:T(8,128)} async-done(((f32[24,8,512]{2,1,0:T(8,128)}), f32[24,128,512]{2,1,0:T(8,128)}) %all-gather.4.cloned.1.call-update) | async-done | bytes 6291472 | tf_op jit(solution)/shard_map/all_gather | solution.py:47
  700.8 1.6 slice-done
  702.4 1.1 dynamic-slice_select_fusion
  704.6 3.5 broadcast_in_dim.109
  708.1 51.8 %scatter_fusion = f32[24,128,4,128]{3,1,2,0:T(8,128)} fusion(f32[24,128,4,128]{3,1,2,0:T(8,128)} %broadcast_in_dim.109, s32[256]{0:T(256)S(1)} %reshape.583, f32[256,128,128]{2,1,0:T(8,128)} %bitcast.23), kind=kCustom, calls=%fused_computation.1 | custom fusion | flops 4194304 | bytes 50333696 | tf_op jit(solution)/shard_map/scatter-add | solution.py:113
  759.9 10.5 %copy.68 = f32[24,128,4,128]{3,2,1,0:T(4,128)} copy(f32[24,128,4,128]{3,1,2,0:T(8,128)} %scatter_fusion) | data formatting | bytes 12582912 | tf_op jit(solution)/shard_map/scatter-add | solution.py:113
  770.4 18.2 %all-reduce.3.cloned.1.call-done = f32[512,512]{1,0:T(8,128)} async-done(((f32[512,512]{1,0:T(8,128)}), f32[512,512]{1,0:T(8,128)}) %all-reduce.3.cloned.1.call-update) | async-done | bytes 1048592 | tf_op jit(solution)/shard_map/psum | solution.py:15
  788.6 16.1 %bitcast_subtract_fusion.1 = f32[3072,512]{1,0:T(8,128)} fusion(f32[384,8,4,128]{3,2,1,0:T(4,128)} %bitcast.222, f32[3072,512]{1,0:T(8,128)} %bitcast.229, f32[512,512]{1,0:T(8,128)} %all-reduce.3.cloned.1.call-done), kind=kOutput, calls=%fused_computation.9 | convolution fusion | flops 9665249280 | bytes 19922944 | tf_op jit(solution)/shard_map/dot_general | solution.py:117
  804.7 7.5 reshape.532
  (133 shorter events, 22.8 us)
Async XLA Ops:
  8.0 341.5 %all-gather.6.cloned.1.call-start = ((), (), s32[]{:S(2)}) async-start(), calls=%async_computation.3 | async-start | bytes 18874368 | tf_op jit(solution)/shard_map/all_gather | solution.py:60
  8.1 5.4 copy-start.3
  106.4 45.1 %copy-start.4 = (f32[512,512]{1,0:T(8,128)}, f32[512,512]{1,0:T(8,128)S(1)}, u32[]{:S(2)}) copy-start(f32[512,512]{1,0:T(8,128)S(1)} %get-tuple-element.206) | copy-start | bytes 3145732
  145.7 5.7 copy-start
  157.9 1.0 copy-start.1
  159.1 2.1 copy-start.7
  159.2 4.8 copy-start.8
  168.6 1.0 copy-start.5
  435.0 8.2 %copy-start.2 = (f32[512,512]{1,0:T(8,128)S(1)}, f32[512,512]{1,0:T(8,128)}, u32[]{:S(2)}) copy-start(f32[512,512]{1,0:T(8,128)} %get-tuple-element.73) | copy-start | bytes 3145732
  435.0 269.6 %all-to-all-start = ((f32[128,2,128,128]{3,2,1,0:T(8,128)}), f32[128,2,128,128]{3,2,1,0:T(8,128)}, u32[]{:S(2)}, u32[]{:S(2)}) async-start(f32[128,2,128,128]{3,2,1,0:T(8,128)} %broadcast_select_fusion), calls=%async_computation | async-start | bytes 33554432 | tf_op jit(solution)/shard_map/all_to_all | solution.py:103
  441.9 50.4 %copy-start.6 = (f32[24,1,1,1,8,512]{5,4,3,2,1,0:T(8,128)S(1)}, f32[24,1,1,1,8,512]{5,4,3,2,1,0:T(8,128)}, u32[]{:S(2)}) copy-start(f32[24,1,1,1,8,512]{5,4,3,2,1,0:T(8,128)} %param.11) | copy-start | bytes 1179652
  441.9 258.9 %all-gather.4.cloned.1.call-start = ((), (), s32[]{:S(2)}) async-start(), calls=%async_computation.1 | async-start | bytes 6684672 | tf_op jit(solution)/shard_map/all_gather | solution.py:47
  495.3 293.3 %all-reduce.3.cloned.1.call-start = ((), (), s32[]{:S(2)}) async-start(), calls=%async_computation.2 | async-start | bytes 2097152 | tf_op jit(solution)/shard_map/psum | solution.py:15
  700.8 1.6 slice-start
Sparse Core Ops, SparseCore 0:
  160.9 188.6 all-gather.5
  703.6 84.9 all-reduce.2
Sparse Core Ops, SparseCore 1:
  495.4 205.4 all-gather.3
where the time goes:
time: 830 us; the launch traced here: 820 us
  waiting for transfers between devices  313 us (38%)
  other arithmetic  309 us (37%)
  local copies, waits for them, and re-layouts  109 us (13%)
  matrix products  60.3 us (7%)
  between operations  21.3 us (3%)
    all_gather x1, waiting for transfers between devices, per_device(): lax.all_gather(solved.reshape(parent_row_blocks, sub_rows, panel_width),...  205 us
    all_gather x1, waiting for transfers between devices, per_device(): everyone = lax.all_gather(leading[None], 'row', axis=0, tiled=True)  89 us
    another operation x14, other arithmetic, per_device(): pivot_lower_factor = jnp.linalg.cholesky(parent_diag)  80.7 us
    another operation x14, other arithmetic, per_device(): child_low = jnp.linalg.cholesky(child_diag[0])  78.9 us
    scatter-add x1, other arithmetic, per_device(): assembled_front.at[target_rows, :, target_cols, :].add(arrived, mode='drop')  51.8 us
    another operation x2, other arithmetic, per_device(): jax.scipy.linalg.solve_triangular(pivot_lower_factor, own_rows.T, lower=T...  40.6 us
    another operation x3, other arithmetic, per_device(): jax.scipy.linalg.solve_triangular(child_low, child_rows.T, lower=True)  39.4 us
    unnamed x24, local copies, waits for them, and re-layouts  28.3 us
  transfers between devices with their start and end apart: 4, of which 3 were waited for; matrix products, arithmetic and copies ran while one was open for 26% of the time, Pallas kernels for 0%

commit v1 on v0

--- a/solution.py
+++ b/solution.py
@@ -57,7 +57,9 @@
     child_rows = child_panel.reshape(-1, panel_width)
     child_factor = jax.scipy.linalg.solve_triangular(child_low, child_rows.T, lower=True).T
     leading = child_factor[: col_local * BLOCK_EXTENT]
-    everyone = lax.all_gather(leading[None], "row", axis=0, tiled=True)
+    everyone = jnp.concatenate(
+        lax.all_to_all(jnp.stack([leading[None]] * lax.axis_size("row")), "row", 0, 0), axis=0
+    )
     child_columns = lax.dynamic_index_in_dim(everyone, col_id, axis=0, keepdims=False)
     schur_part = child_window.reshape(row_local * BLOCK_EXTENT, col_local * BLOCK_EXTENT) - jnp.dot(
         child_factor, child_columns.T, precision=highest

time: 830 us -> 895 us (1.078)
  starting transfers between devices: 6.99 us -> 82.9 us
  local copies, waits for them, and re-layouts: 109 us -> 91 us
  matrix products: 60.3 us -> 72.1 us
    all_gather x1 -> x0, waiting for transfers between devices: 89 us -> none  [per_device(): everyone = lax.all_gather(leading[None], 'row', axis=0, tiled=True)]
    all_to_all x0 -> x1, waiting for transfers between devices: none -> 86 us  [per_device(): lax.all_to_all(jnp.stack([leading[None]] * lax.axis_size('row')), 'row',...]
    all_to_all x1, starting transfers between devices: 6.87 us -> 74.8 us  [per_device(): lax.all_to_all(outgoing.reshape(-1, per_row * per_col, BLOCK_EXTENT, BLOC...]
    unnamed x24 -> x23, local copies, waits for them, and re-layouts: 28.3 us -> 6.96 us
    dot_general x1, matrix products: 20.5 us -> 32.4 us  [per_device(): jnp.dot(child_factor, child_columns.T, precision=highest)]
    another operation x24 -> x25, local copies, waits for them, and re-layouts: 16.3 us -> 25.8 us
    dynamic_slice x1 -> x0, local copies, waits for them, and re-layouts: 9.43 us -> none  [per_device(): lax.dynamic_index_in_dim(everyone, col_id, axis=0, keepdims=False)]
  transfers between devices with their start and end apart: 4 -> 4, of which waited for: 3 -> 3; matrix products, arithmetic and copies ran while one was open for 26% -> 25% of each run, Pallas kernels for 0% -> 0%
where the time goes in v1:
time: 895 us; the launch traced here: 885 us
  waiting for transfers between devices  310 us (35%)
  other arithmetic  308 us (34%)
  local copies, waits for them, and re-layouts  91 us (10%)
  starting transfers between devices  82.9 us (9%)
  matrix products  72.1 us (8%)
  between operations  20 us (2%)
    all_gather x1, waiting for transfers between devices, per_device(): lax.all_gather(solved.reshape(parent_row_blocks, sub_rows, panel_width),...  205 us
    all_to_all x1, waiting for transfers between devices, per_device(): lax.all_to_all(jnp.stack([leading[None]] * lax.axis_size('row')), 'row',...  86 us
    another operation x14, other arithmetic, per_device(): pivot_lower_factor = jnp.linalg.cholesky(parent_diag)  80.6 us
    another operation x14, other arithmetic, per_device(): child_low = jnp.linalg.cholesky(child_diag[0])  78.6 us
    all_to_all x1, starting transfers between devices, per_device(): lax.all_to_all(outgoing.reshape(-1, per_row * per_col, BLOCK_EXTENT, BLOC...  74.8 us
    scatter-add x1, other arithmetic, per_device(): assembled_front.at[target_rows, :, target_cols, :].add(arrived, mode='drop')  51.8 us
    another operation x2, other arithmetic, per_device(): jax.scipy.linalg.solve_triangular(pivot_lower_factor, own_rows.T, lower=T...  40.6 us
    another operation x3, other arithmetic, per_device(): jax.scipy.linalg.solve_triangular(child_low, child_rows.T, lower=True)  39.4 us
  transfers between devices with their start and end apart: 4, of which 3 were waited for; matrix products, arithmetic and copies ran while one was open for 25% of the time, Pallas kernels for 0%

profile of v1, /device:TPU:0, one launch (start us, length us, event | category | flops | bytes accessed | tf_op | source)
XLA Modules:
  0.0 884.8 jit_solution(13484040815482824368)
XLA Ops:
  7.2 5.4 copy.80
  13.2 11.7 %cholesky.286 = f32[128,128]{1,0:T(8,128)S(1)} custom-call(f32[128,128]{1,0:T(8,128)S(1)} %cholesky.426), custom_call_target="Cholesky" | custom-call | tf_op jit(solution)/shard_map/jit(cholesky)/cholesky | solution.py:56
  25.1 9.8 %custom-call.37 = f32[1,128,128]{1,2,0:T(8,128)S(1)} custom-call(f32[1,128,128]{2,1,0:T(8,128)S(1)} %get-tuple-element.91), custom_call_target="InvertDiagBlocksLowerTriangular" | custom-call | tf_op jit(solution)/shard_map/jit(cholesky)/cholesky | solution.py:56
  35.6 11.7 %cholesky.305 = f32[128,128]{1,0:T(8,128)S(1)} custom-call(f32[128,128]{1,0:T(8,128)S(1)} %cholesky.430), custom_call_target="Cholesky" | custom-call | tf_op jit(solution)/shard_map/jit(cholesky)/cholesky | solution.py:56
  47.3 10.0 %custom-call.38 = f32[1,128,128]{1,2,0:T(8,128)S(1)} custom-call(f32[1,128,128]{2,1,0:T(8,128)S(1)} %get-tuple-element.88), custom_call_target="InvertDiagBlocksLowerTriangular" | custom-call | tf_op jit(solution)/shard_map/jit(cholesky)/cholesky | solution.py:56
  57.9 11.7 %cholesky.326 = f32[128,128]{1,0:T(8,128)S(1)} custom-call(f32[128,128]{1,0:T(8,128)S(1)} %cholesky.435), custom_call_target="Cholesky" | custom-call | tf_op jit(solution)/shard_map/jit(cholesky)/cholesky | solution.py:56
  69.7 9.8 %custom-call.39 = f32[1,128,128]{1,2,0:T(8,128)S(1)} custom-call(f32[1,128,128]{2,1,0:T(8,128)S(1)} %get-tuple-element.85), custom_call_target="InvertDiagBlocksLowerTriangular" | custom-call | tf_op jit(solution)/shard_map/jit(cholesky)/cholesky | solution.py:56
  80.1 11.7 %cholesky.343 = f32[128,128]{1,0:T(8,128)S(1)} custom-call(f32[128,128]{1,0:T(8,128)S(1)} %convolution_subtract_fusion.10), custom_call_target="Cholesky" | custom-call | tf_op jit(solution)/shard_map/jit(cholesky)/cholesky | solution.py:56
  96.6 8.9 %while.2 = (s32[]{:T(128)}, f32[512,512]{1,0:T(8,128)S(1)}, s32[4,2]{0,1:T(2,128)S(1)}, f32[4,128,128]{2,1,0:T(8,128)S(1)}, s32[]{:T(128)}) while((s32[]{:T(128)}, f32[512,512]{1,0:T(8,128)S(1)}, s32[4,2]{0,1:T(2,128)S(1)}, f32[4,128,128]{2,1,0:T(8,128)S(1)}, s32[]{:T(128)}) %tuple.70), condition=%wide.while_cond, body=%wide.while_body.sunk | while | flops 2 | bytes 131189 | solution.py:58
  97.7 1.4 bitcast_dynamic-update-slice_fusion.4
  99.8 1.4 bitcast_dynamic-update-slice_fusion.4
  101.9 1.4 bitcast_dynamic-update-slice_fusion.4
  104.0 1.4 bitcast_dynamic-update-slice_fusion.4
  105.5 39.3 %custom-call.28 = f32[4,128,128]{1,2,0:T(8,128)S(1)} custom-call(f32[4,128,128]{2,1,0:T(8,128)S(1)} %get-tuple-element.11), custom_call_target="InvertDiagBlocksLowerTriangular" | custom-call | tf_op jit(solution)/shard_map/jit(_solve_triangular)/triangular_solve | solution.py:58
  144.8 2.4 fusion.16
  147.2 2.2 convolution_subtract_fusion.1
  149.5 1.1 fusion.58
  150.6 1.3 convolution_subtract_fusion
  151.8 1.1 fusion.56
  152.9 3.0 fusion.7
  155.9 1.0 fusion.55
  156.9 1.0 copy-done.1
  158.2 1.6 slice.169
  159.8 2.9 copy.71
  162.7 9.5 %stack.3 = f32[8,1,1024,512]{3,2,1,0:T(8,128)} broadcast(f32[1024,512]{1,0:T(8,128)} %copy.71), dimensions={2,3} | broadcast | bytes 18874368 | tf_op jit(solution)/shard_map/stack | solution.py:61
  172.2 8.0 all-to-all-start
  183.7 2.5 copy.75
  186.2 1.8 fusion.19
  188.0 1.0 copy-done.5
  189.0 11.7 %cholesky.358 = f32[128,128]{1,0:T(8,128)S(1)} custom-call(f32[128,128]{1,0:T(8,128)S(1)} %cholesky.439), custom_call_target="Cholesky" | custom-call | tf_op jit(solution)/shard_map/jit(cholesky)/cholesky | solution.py:42
  200.7 1.1 cholesky.384
  201.8 9.8 %custom-call.40 = f32[1,128,128]{1,2,0:T(8,128)S(1)} custom-call(f32[1,128,128]{2,1,0:T(8,128)S(1)} %get-tuple-element.81), custom_call_target="InvertDiagBlocksLowerTriangular" | custom-call | tf_op jit(solution)/shard_map/jit(cholesky)/cholesky | solution.py:42
  211.7 1.9 constant_dynamic-update-slice_fusion.2
  213.6 1.2 convolution_subtract_fusion.2
  214.8 11.7 %cholesky.377 = f32[128,128]{1,0:T(8,128)S(1)} custom-call(f32[128,128]{1,0:T(8,128)S(1)} %cholesky.443), custom_call_target="Cholesky" | custom-call | tf_op jit(solution)/shard_map/jit(cholesky)/cholesky | solution.py:42
  227.2 10.2 %custom-call.41 = f32[1,128,128]{1,2,0:T(8,128)S(1)} custom-call(f32[1,128,128]{2,1,0:T(8,128)S(1)} %get-tuple-element.78), custom_call_target="InvertDiagBlocksLowerTriangular" | custom-call | tf_op jit(solution)/shard_map/jit(cholesky)/cholesky | solution.py:42
  238.3 1.4 convolution_subtract_fusion.4
  239.7 11.7 %cholesky.398 = f32[128,128]{1,0:T(8,128)S(1)} custom-call(f32[128,128]{1,0:T(8,128)S(1)} %cholesky.448), custom_call_target="Cholesky" | custom-call | tf_op jit(solution)/shard_map/jit(cholesky)/cholesky | solution.py:42
  252.1 9.8 %custom-call.42 = f32[1,128,128]{1,2,0:T(8,128)S(1)} custom-call(f32[1,128,128]{2,1,0:T(8,128)S(1)} %get-tuple-element.75), custom_call_target="InvertDiagBlocksLowerTriangular" | custom-call | tf_op jit(solution)/shard_map/jit(cholesky)/cholesky | solution.py:42
  262.8 1.4 convolution_subtract_fusion.9
  264.2 11.7 %cholesky.415 = f32[128,128]{1,0:T(8,128)S(1)} custom-call(f32[128,128]{1,0:T(8,128)S(1)} %convolution_subtract_fusion.9), custom_call_target="Cholesky" | custom-call | tf_op jit(solution)/shard_map/jit(cholesky)/cholesky | solution.py:42
  279.8 86.0 %all-to-all-done = f32[8,1,1024,512]{3,2,1,0:T(8,128)} async-done(((f32[8,1,1024,512]{3,2,1,0:T(8,128)}), f32[8,1,1024,512]{3,2,1,0:T(8,128)}, u32[]{:S(2)}, u32[]{:S(2)}) %all-to-all-start) | async-done | bytes 16777248 | tf_op jit(solution)/shard_map/all_to_all | solution.py:61
  365.9 32.4 %fusion = f32[256,8,8,128]{3,1,2,0:T(8,128)S(1)} fusion(f32[256,8,8,128]{3,2,1,0:T(8,128)} %bitcast.224, f32[128,2048]{1,0:T(8,128)} %copy-done.1, f32[128,2048]{1,0:T(8,128)S(1)} %fusion.56, f32[128,2048]{1,0:T(8,128)S(1)} %fusion.58, f32[128,2048]{1,0:T(8,128)S(1)} %fusion.16, f32[8,1,1024,512]{3,2,1,0:T(8,128)} %all-to-all-done, s32[]{:T(128)S(6)} %select_n.220), kind=kOutput, calls=%fused_computation.7 | convolution fusion | flops 12890144768 | bytes 23068676 | tf_op jit(solution)/shard_map/dot_general | solution.py:64
  398.3 2.1 copy.83
  400.4 4.7 copy.73
  405.0 16.0 %gather_fusion = f32[256,128,128]{2,1,0:T(8,128)} fusion(f32[16,128,8,128]{3,1,2,0:T(8,128)} %copy.73, s32[256]{0:T(256)S(1)} %reshape.580), kind=kCustom, calls=%fused_computation | custom fusion | bytes 33556480 | tf_op jit(solution)/shard_map/gather | solution.py:104
  421.0 11.4 %broadcast_select_fusion = f32[128,2,128,128]{3,2,1,0:T(8,128)} fusion(f32[128,2,128,128]{3,2,1,0:T(8,128)} %bitcast.216, pred[128,2]{1,0:T(8,128)(4,1)S(1)} %bitcast.233), kind=kLoop, calls=%fused_computation.8 | loop fusion | flops 4194304 | bytes 33554688 | tf_op jit(solution)/shard_map/select_n | solution.py:104
  432.4 74.8 %all-to-all-start.1 = ((f32[128,2,128,128]{3,2,1,0:T(8,128)}), f32[128,2,128,128]{3,2,1,0:T(8,128)}, u32[]{:S(2)}, u32[]{:S(2)}) async-start(f32[128,2,128,128]{3,2,1,0:T(8,128)} %broadcast_select_fusion), calls=%async_computation.1 | async-start | bytes 33554432 | tf_op jit(solution)/shard_map/all_to_all | solution.py:105
  508.6 1.2 fusion.20
  509.9 8.4 while.3
  510.9 1.4 bitcast_dynamic-update-slice_fusion.5
  512.9 1.4 bitcast_dynamic-update-slice_fusion.5
  514.9 1.4 bitcast_dynamic-update-slice_fusion.5
  516.9 1.4 bitcast_dynamic-update-slice_fusion.5
  518.3 39.3 %custom-call.29 = f32[4,128,128]{1,2,0:T(8,128)S(1)} custom-call(f32[4,128,128]{2,1,0:T(8,128)S(1)} %get-tuple-element.19), custom_call_target="InvertDiagBlocksLowerTriangular" | custom-call | tf_op jit(solution)/shard_map/jit(_solve_triangular)/triangular_solve | solution.py:44
  560.8 205.2 %all-gather.2.cloned.1.call-done = f32[24,128,512]{2,1,0:T(8,128)} async-done(((f32[24,8,512]{2,1,0:T(8,128)}), f32[24,128,512]{2,1,0:T(8,128)}) %all-gather.2.cloned.1.call-update) | async-done | bytes 6291472 | tf_op jit(solution)/shard_map/all_gather | solution.py:47
  766.0 1.8 slice.172
  767.8 1.1 dynamic-slice_select_fusion
  770.1 3.5 broadcast_in_dim.106
  773.5 51.8 %scatter_fusion = f32[24,128,4,128]{3,1,2,0:T(8,128)} fusion(f32[24,128,4,128]{3,1,2,0:T(8,128)} %broadcast_in_dim.106, s32[256]{0:T(256)S(1)} %reshape.588, f32[256,128,128]{2,1,0:T(8,128)} %bitcast.24), kind=kCustom, calls=%fused_computation.1 | custom fusion | flops 4194304 | bytes 50333696 | tf_op jit(solution)/shard_map/scatter-add | solution.py:115
  825.4 10.5 %copy.74 = f32[24,128,4,128]{3,2,1,0:T(4,128)} copy(f32[24,128,4,128]{3,1,2,0:T(8,128)} %scatter_fusion) | data formatting | bytes 12582912 | tf_op jit(solution)/shard_map/scatter-add | solution.py:115
  835.8 18.3 %all-reduce.3.cloned.1.call-done = f32[512,512]{1,0:T(8,128)} async-done(((f32[512,512]{1,0:T(8,128)}), f32[512,512]{1,0:T(8,128)}) %all-reduce.3.cloned.1.call-update) | async-done | bytes 1048592 | tf_op jit(solution)/shard_map/psum | solution.py:15
  854.1 16.1 %bitcast_subtract_fusion.1 = f32[3072,512]{1,0:T(8,128)} fusion(f32[384,8,4,128]{3,2,1,0:T(4,128)} %bitcast.218, f32[3072,512]{1,0:T(8,128)} %bitcast.223, f32[512,512]{1,0:T(8,128)} %all-reduce.3.cloned.1.call-done), kind=kOutput, calls=%fused_computation.9 | convolution fusion | flops 9665249280 | bytes 19922944 | tf_op jit(solution)/shard_map/dot_general | solution.py:119
  870.2 7.5 reshape.537
  (131 shorter events, 23.7 us)
Async XLA Ops:
  7.2 5.5 copy-start.3
  105.5 45.1 %copy-start.4 = (f32[512,512]{1,0:T(8,128)}, f32[512,512]{1,0:T(8,128)S(1)}, u32[]{:S(2)}) copy-start(f32[512,512]{1,0:T(8,128)S(1)} %get-tuple-element.204) | copy-start | bytes 3145732
  144.8 5.7 copy-start
  156.9 1.0 copy-start.1
  172.2 8.5 copy-start.7
  172.2 11.2 %copy-start.8 = (s32[2]{0:T(128)S(1)}, s32[2]{0:T(128)}, u32[]{:S(2)}) copy-start(s32[2]{0:T(128)} %constant.261.clone.1) | copy-start | bytes 28
  172.2 193.7 %all-to-all-start = ((f32[8,1,1024,512]{3,2,1,0:T(8,128)}), f32[8,1,1024,512]{3,2,1,0:T(8,128)}, u32[]{:S(2)}, u32[]{:S(2)}) async-start(f32[8,1,1024,512]{3,2,1,0:T(8,128)} %stack.3), calls=%async_computation | async-start | bytes 33554432 | tf_op jit(solution)/shard_map/all_to_all | solution.py:61
  188.0 1.0 copy-start.5
  432.4 76.2 %copy-start.2 = (f32[512,512]{1,0:T(8,128)S(1)}, f32[512,512]{1,0:T(8,128)}, u32[]{:S(2)}) copy-start(f32[512,512]{1,0:T(8,128)} %get-tuple-element.73) | copy-start | bytes 3145732
  432.4 125.2 %copy-start.6 = (f32[24,1,1,1,8,512]{5,4,3,2,1,0:T(8,128)S(1)}, f32[24,1,1,1,8,512]{5,4,3,2,1,0:T(8,128)}, u32[]{:S(2)}) copy-start(f32[24,1,1,1,8,512]{5,4,3,2,1,0:T(8,128)} %param.11) | copy-start | bytes 1179652
  432.4 337.6 %all-to-all-start.1 = ((f32[128,2,128,128]{3,2,1,0:T(8,128)}), f32[128,2,128,128]{3,2,1,0:T(8,128)}, u32[]{:S(2)}, u32[]{:S(2)}) async-start(f32[128,2,128,128]{3,2,1,0:T(8,128)} %broadcast_select_fusion), calls=%async_computation.1 | async-start | bytes 33554432 | tf_op jit(solution)/shard_map/all_to_all | solution.py:105
  507.3 258.7 %all-gather.2.cloned.1.call-start = ((), (), s32[]{:S(2)}) async-start(), calls=%async_computation.2 | async-start | bytes 6684672 | tf_op jit(solution)/shard_map/all_gather | solution.py:47
  560.6 293.5 %all-reduce.3.cloned.1.call-start = ((), (), s32[]{:S(2)}) async-start(), calls=%async_computation.3 | async-start | bytes 2097152 | tf_op jit(solution)/shard_map/psum | solution.py:15
Sparse Core Ops, SparseCore 0:
  560.7 205.2 all-gather.1
  769.0 85.0 all-reduce.2
